TPU v7x, 32 devices: a whole 2x2x4 slice. The times are simulated.
32 devices in a mesh: slab: 8 (over y, x, core), view: 4 (over z).
Axes of the slice: x: 2, y: 2, z: 4, core: 2. Of those that a mesh axis runs over, the one named last changes fastest.
Arguments:
- estimate: float32 [4, 1024, 1024], P(None, 'slab'), may hold values from 0.5 to 2
- views: float32 [4, 4, 1024, 1024], P('view', None, 'slab'), may hold values from 0.25 to 4
- psf: float32 [4, 1024, 1024], P('view', 'slab'), as said below
- pattern_mult: int32 [4, 8], P('view'), may hold values from 0 to 63
- pattern_shift: int32 [4, 8], P('view'), may hold values from 0 to 127
- interp: float32 [4, 8, 128], P('view'), may hold values from 0.05 to 0.45
Outputs:
- updated: float32 [4, 1024, 1024], P(None, 'slab')
Inputs may be any that keep to these rules, and one draw needn't show every extreme that they name: `psf`: every entry is positive.
All inputs are finite; a program needn't handle non-finite values.
Results may differ from a plain program's by a relative error of at most 0.0001.
Values sent between devices are 32-bit elements; how exact they have to be, the bound alone decides.
No kernel may reach another device: no remote copies, remote signals or barrier semaphores. Data moves between devices by JAX's collectives and lax.ppermute only.
A program may use at most 128 MiB of HBM per device.

v0:
```python
import math
import jax
import jax.numpy as jnp
from jax import lax
from jax.sharding import PartitionSpec as P

highest = lax.Precision.HIGHEST


def block_matrix(multiplier, shifting, weights):
    positions = jnp.arange(128, dtype=jnp.int32)
    first_col = ((2 * multiplier[:, None] + 1) * positions[None, :] + shifting[:, None]) % 128
    second_col = (first_col + 1) % 128
    columns = positions[None, None, :]
    lower = (columns == first_col[:, :, None]).astype(jnp.float32)
    upper = (columns == second_col[:, :, None]).astype(jnp.float32)
    return (1.0 - weights)[:, :, None] * lower + weights[:, :, None] * upper


def angle_tables(rows, cols, length):
    row_index = lax.iota(jnp.int32, rows)[:, None]
    col_index = lax.iota(jnp.int32, cols)[None, :]
    angles = (row_index * col_index % length).astype(jnp.float32) * (2.0 * math.pi / length)
    return (jnp.cos(angles), jnp.sin(angles))


def unit_root(numerator, length):
    angle = 2.0 * math.pi * numerator / length
    return (round(math.cos(angle), 15), round(math.sin(angle), 15))


def small_stage(real_part, imag_part, axis, direction):
    count = real_part.shape[axis]

    def part(array, index):
        return lax.index_in_dim(array, index, axis, keepdims=False)

    real_in = [part(real_part, index) for index in range(count)]
    imag_in = None if imag_part is None else [part(imag_part, index) for index in range(count)]
    real_out, imag_out = ([], [])
    for out_index in range(count):
        real_sum, imag_sum = (None, None)
        for in_index in range(count):
            cosine, sine = unit_root(in_index * out_index, count)
            sine = direction * sine
            terms_real = []
            terms_imag = []
            if cosine != 0.0:
                terms_real.append(cosine * real_in[in_index])
                if imag_in is not None:
                    terms_imag.append(cosine * imag_in[in_index])
            if sine != 0.0:
                terms_imag.append(sine * real_in[in_index])
                if imag_in is not None:
                    terms_real.append(-sine * imag_in[in_index])
            for term in terms_real:
                real_sum = term if real_sum is None else real_sum + term
            for term in terms_imag:
                imag_sum = term if imag_sum is None else imag_sum + term
        if imag_sum is None:
            imag_sum = jnp.zeros_like(real_sum)
        real_out.append(real_sum)
        imag_out.append(imag_sum)
    return (jnp.stack(real_out, axis), jnp.stack(imag_out, axis))


def complex_times(real_part, imag_part, cosine, sine_table):
    return (
        real_part * cosine - imag_part * sine_table,
        real_part * sine_table + imag_part * cosine,
    )


def block_dft_matrix(length, direction):
    cosine, sine = angle_tables(length, length, length)
    sine = direction * sine
    top = jnp.concatenate([cosine, sine], 1)
    bottom = jnp.concatenate([-sine, cosine], 1)
    return jnp.concatenate([top, bottom], 0)


def large_stage(real_part, imag_part, axis, direction):
    length = real_part.shape[axis]
    if imag_part is None:
        imag_part = jnp.zeros_like(real_part)
    joined = jnp.concatenate([real_part, imag_part], axis)
    matrix = block_dft_matrix(length, direction)
    if axis == joined.ndim - 1:
        out = jnp.einsum("...j,jn->...n", joined, matrix, precision=highest)
    else:
        out = jnp.einsum("rkjz,jn->rknz", joined, matrix, precision=highest)
    return (
        lax.slice_in_dim(out, 0, length, axis=axis),
        lax.slice_in_dim(out, length, 2 * length, axis=axis),
    )


def factored(real_part, imag_part, axis, direction, forward, want_imag=True):
    length = real_part.shape[axis]
    second = 128
    first = length // second
    outer = real_part.shape
    shape = outer[:axis] + (first, second) + outer[axis + 1 :]
    real_part = real_part.reshape(shape)
    if imag_part is not None:
        imag_part = imag_part.reshape(shape)
    twist_cos, twist_sin = angle_tables(first, second, length)
    if axis == 1:
        twist_cos = twist_cos[:, :, None]
        twist_sin = twist_sin[:, :, None]
    twist_sin = direction * twist_sin
    if forward:
        real_part, imag_part = small_stage(real_part, imag_part, axis, direction)
        real_part, imag_part = complex_times(real_part, imag_part, twist_cos, twist_sin)
        real_part, imag_part = large_stage(real_part, imag_part, axis + 1, direction)
    else:
        real_part, imag_part = large_stage(real_part, imag_part, axis + 1, direction)
        real_part, imag_part = complex_times(real_part, imag_part, twist_cos, twist_sin)
        real_part, imag_part = small_stage(real_part, imag_part, axis, direction)
    return (real_part.reshape(outer), imag_part.reshape(outer))


def to_columns(real_part, imag_part):
    depth_real, depth_imag = factored(real_part, imag_part, 2, -1.0, True)
    rows = depth_real.shape[0]
    stacked = jnp.concatenate([depth_real, depth_imag], 0)
    moved = lax.all_to_all(stacked, "slab", split_axis=2, concat_axis=1, tiled=True)
    return factored(moved[:rows], moved[rows:], 1, -1.0, True)


def to_planes(real_part, imag_part):
    width_real, width_imag = factored(real_part, imag_part, 1, 1.0, False)
    rows = width_real.shape[0]
    stacked = jnp.concatenate([width_real, width_imag], 0)
    moved = lax.all_to_all(stacked, "slab", split_axis=1, concat_axis=2, tiled=True)
    return factored(moved[:rows], moved[rows:], 2, 1.0, False)


def pack_pairs(volume):
    return (volume[0::2], volume[1::2])


def unpack_pairs(real_part, imag_part):
    pairs, width, depth = real_part.shape
    return jnp.stack([real_part, imag_part], 1).reshape(2 * pairs, width, depth)


def general_shards(estimate, views, psf, pattern_mult, pattern_shift, interp):
    row_count, slab_width, depth = estimate.shape
    blocks = block_matrix(pattern_mult[0], pattern_shift[0], interp[0])
    block_count = depth // 128
    shaped = estimate.reshape(row_count, slab_width, block_count, 128)
    sampled = jnp.einsum("bij,yxbj->yxbi", blocks, shaped, precision=highest).reshape(
        row_count, slab_width, depth
    )
    packed_real, packed_imag = pack_pairs(sampled)
    packed_real = jnp.concatenate([packed_real, psf], 0)
    packed_imag = jnp.concatenate([packed_imag, jnp.zeros_like(psf)], 0)
    spectra_real, spectra_imag = to_columns(packed_real, packed_imag)
    scaling = 1.0 / (spectra_real.shape[1] * depth)
    transfer_real = spectra_real[-1:] * scaling
    transfer_imag = spectra_imag[-1:] * scaling
    spectra_real = spectra_real[:-1]
    spectra_imag = spectra_imag[:-1]
    filtered_real = spectra_real * transfer_real - spectra_imag * transfer_imag
    filtered_imag = spectra_real * transfer_imag + spectra_imag * transfer_real
    blurred = unpack_pairs(*to_planes(filtered_real, filtered_imag))
    quotient = views[0] / blurred
    packed_real, packed_imag = pack_pairs(quotient)
    spectra_real, spectra_imag = to_columns(packed_real, packed_imag)
    filtered_real = spectra_real * transfer_real + spectra_imag * transfer_imag
    filtered_imag = spectra_imag * transfer_real - spectra_real * transfer_imag
    smeared = unpack_pairs(*to_planes(filtered_real, filtered_imag))
    correction = jnp.einsum(
        "bij,yxbi->yxbj",
        blocks,
        smeared.reshape(row_count, slab_width, block_count, 128),
        precision=highest,
    ).reshape(row_count, slab_width, depth)
    log_terms = jnp.log(correction)
    view_count = lax.axis_size("view")
    summed = lax.psum(log_terms, "view")
    return estimate * jnp.exp(summed / view_count)


def swap_halves(joined):
    half = joined.shape[-1] // 2
    return jnp.concatenate([-joined[..., half:], joined[..., :half]], -1)


def butterflies(parts, direction, turn):
    count = len(parts)
    if count == 1:
        return parts
    even = butterflies(parts[0::2], direction, turn)
    odd = butterflies(parts[1::2], direction, turn)
    out = [None] * count
    for index in range(count // 2):
        cosine, sine = unit_root(index, count)
        sine = direction * sine
        value = odd[index]
        if sine == 0.0:
            rotated = value if cosine > 0 else -value
        elif cosine == 0.0:
            rotated = turn(value) if sine > 0 else -turn(value)
        else:
            rotated = cosine * value + sine * turn(value)
        out[index] = even[index] + rotated
        out[index + count // 2] = even[index] - rotated
    return out


def lead_stage(joined, direction):
    count = joined.shape[0]
    parts = [joined[index] for index in range(count)]
    return jnp.stack(butterflies(parts, direction, swap_halves), 0)


def joined_twist(joined, length, direction, lanes):
    first, second = (joined.shape[0], joined.shape[-1] // 2 if lanes else joined.shape[2])
    cosine, sine = angle_tables(first, second, length)
    sine = direction * sine
    if lanes:
        cosine = jnp.concatenate([cosine, cosine], 1)[:, None, None, :]
        sine = jnp.concatenate([sine, sine], 1)[:, None, None, :]
    else:
        cosine = cosine[:, None, :, None]
        sine = sine[:, None, :, None]
    return joined * cosine + swap_halves(joined) * sine


def lane_stage(joined, direction):
    length = joined.shape[-1] // 2
    matrix = block_dft_matrix(length, direction)
    return jnp.einsum("...j,jn->...n", joined, matrix, precision=lax.Precision.HIGH)


def row_stage(joined, direction):
    length = joined.shape[2]
    cosine, sine = angle_tables(length, length, length)
    matrix = jnp.concatenate([cosine, direction * sine], 0)
    both = jnp.concatenate([joined, swap_halves(joined)], 2)
    return jnp.einsum("krjl,jm->krml", both, matrix, precision=lax.Precision.HIGH)


def depth_forward(joined, depth):
    joined = lead_stage(joined, -1.0)
    joined = joined_twist(joined, depth, -1.0, True)
    return lane_stage(joined, -1.0)


def depth_inverse(joined, depth):
    joined = lane_stage(joined, 1.0)
    joined = joined_twist(joined, depth, 1.0, True)
    return lead_stage(joined, 1.0)


def width_forward(joined, width):
    joined = lead_stage(joined, -1.0)
    joined = joined_twist(joined, width, -1.0, False)
    return row_stage(joined, -1.0)


def width_inverse(joined, width):
    joined = row_stage(joined, 1.0)
    joined = joined_twist(joined, width, 1.0, False)
    return lead_stage(joined, 1.0)


def joined_times(joined, transfer_real, transfer_imag):
    return joined * transfer_real + swap_halves(joined) * transfer_imag


def to_blocks(volume, block_count):
    rows, width, depth = volume.shape
    lanes = depth // block_count
    parity = [volume[0::2], volume[1::2]]
    return jnp.stack(
        [
            jnp.concatenate(
                [part[:, :, block * lanes : (block + 1) * lanes] for part in parity], -1
            )
            for block in range(block_count)
        ],
        0,
    )


def from_blocks(blocked):
    block_count, pairs, width, lanes = blocked.shape
    half = lanes // 2
    parity = [
        jnp.concatenate(
            [blocked[block, :, :, side * half : (side + 1) * half] for block in range(block_count)],
            -1,
        )
        for side in range(2)
    ]
    return jnp.stack(parity, 1).reshape(2 * pairs, width, block_count * half)


def shards(estimate, views, psf, pattern_mult, pattern_shift, interp):
    row_count, slab_width, depth = estimate.shape
    slab_count = lax.axis_size("slab")
    block_count = depth // 128
    width = slab_width * slab_count
    if not (
        block_count == slab_count
        and slab_width == 128
        and (width // 128 == slab_count)
        and (row_count % 2 == 0)
    ):
        return general_shards(estimate, views, psf, pattern_mult, pattern_shift, interp)
    blocks = block_matrix(pattern_mult[0], pattern_shift[0], interp[0])
    empty = jnp.zeros_like(blocks)
    doubled = jnp.concatenate(
        [jnp.concatenate([blocks, empty], 2), jnp.concatenate([empty, blocks], 2)], 1
    )
    sampled = jnp.einsum(
        "apxl,aml->apxm", to_blocks(estimate, block_count), doubled, precision=lax.Precision.HIGH
    )
    pairs = row_count // 2
    spread = psf.reshape(slab_width, block_count, 128).transpose(1, 0, 2)[:, None]
    spread = jnp.concatenate([spread, jnp.zeros_like(spread)], -1)

    def to_columns_blocked(planes):
        spectra = depth_forward(planes, depth)
        spectra = lax.all_to_all(spectra, "slab", split_axis=0, concat_axis=0, tiled=True)
        return width_forward(spectra, width)

    transfer = to_columns_blocked(spread) * (1.0 / (width * depth))
    spectra = to_columns_blocked(sampled)
    half = transfer.shape[-1] // 2
    transfer_real = jnp.concatenate([transfer[..., :half], transfer[..., :half]], -1)
    transfer_imag = jnp.concatenate([transfer[..., half:], transfer[..., half:]], -1)

    def convolve(spectra, transfer_imag):
        filtered = joined_times(spectra, transfer_real, transfer_imag)
        planes = width_inverse(filtered, width)
        planes = lax.all_to_all(planes, "slab", split_axis=0, concat_axis=0, tiled=True)
        return depth_inverse(planes, depth)

    blurred = convolve(spectra, transfer_imag)
    quotient = to_blocks(views[0], block_count) / blurred
    spectra = depth_forward(quotient, depth)
    spectra = lax.all_to_all(spectra, "slab", split_axis=0, concat_axis=0, tiled=True)
    spectra = width_forward(spectra, width)
    smeared = convolve(spectra, -transfer_imag)
    correction = jnp.einsum("apxm,aml->apxl", smeared, doubled, precision=lax.Precision.HIGH)
    log_terms = from_blocks(jnp.log(correction))
    view_count = lax.axis_size("view")
    summed = lax.psum(log_terms, "view")
    return estimate * jnp.exp(summed / view_count)


def solution(mesh):
    placed = (
        P(None, "slab", None),
        P("view", None, "slab", None),
        P("view", "slab", None),
        P("view", None),
        P("view", None),
        P("view", None, None),
    )
    return jax.shard_map(
        shards, mesh=mesh, in_specs=placed, out_specs=P(None, "slab", None), check_vma=False
    )
```

profile of v0, /device:TPU:0, one launch (start us, length us, event | category | flops | bytes accessed | tf_op | source)
XLA Modules:
  0.0 285.5 jit_solution(3338076680275577387)
XLA Ops:
  6.6 0.3 broadcast_multiply_fusion
  7.2 1.2 copy.41
  9.5 1.6 convolution_bitcast_fusion
  11.1 5.2 %all-to-all-start.1 = ((f32[8,1,128,256]{3,2,1,0:T(8,128)}), f32[8,1,128,256]{3,2,1,0:T(8,128)S(1)}, u32[]{:S(2)}, u32[]{:S(2)}) async-start(f32[8,1,128,256]{3,2,1,0:T(8,128)} %convolution_bitcast_fusion), calls=%async_computation.1 | async-start | bytes 2097152 | tf_op jit(solution)/shard_map/all_to_all | solution.py:328
  16.8 0.4 copy-done.8
  17.5 0.4 copy-done.7
  18.2 0.6 select_add_fusion
  18.8 1.1 fusion.52
  21.4 2.4 fusion.26
  23.8 7.9 %all-to-all-done.1 = f32[8,1,128,256]{3,2,1,0:T(8,128)S(1)} async-done(((f32[8,1,128,256]{3,2,1,0:T(8,128)}), f32[8,1,128,256]{3,2,1,0:T(8,128)S(1)}, u32[]{:S(2)}, u32[]{:S(2)}) %all-to-all-start.1) | async-done | bytes 1048608 | tf_op jit(solution)/shard_map/all_to_all | solution.py:328
  31.7 3.8 %all-to-all-start = ((f32[8,2,128,256]{3,2,1,0:T(8,128)}), f32[8,2,128,256]{3,2,1,0:T(8,128)S(1)}, u32[]{:S(2)}, u32[]{:S(2)}) async-start(f32[8,2,128,256]{3,2,1,0:T(8,128)} %fusion.26), calls=%async_computation | async-start | bytes 4194304 | tf_op jit(solution)/shard_map/all_to_all | solution.py:328
  36.3 0.4 fusion.79
  36.7 0.9 fusion.70
  37.6 1.0 slice_bitcast_fusion.67
  38.6 1.0 maximum_bitcast_fusion.7
  39.7 22.2 %all-to-all-done = f32[8,2,128,256]{3,2,1,0:T(8,128)S(1)} async-done(((f32[8,2,128,256]{3,2,1,0:T(8,128)}), f32[8,2,128,256]{3,2,1,0:T(8,128)S(1)}, u32[]{:S(2)}, u32[]{:S(2)}) %all-to-all-start) | async-done | bytes 2097184 | tf_op jit(solution)/shard_map/all_to_all | solution.py:328
  63.2 0.4 fusion.30
  63.8 1.6 fusion.66
  65.7 1.0 copy-done.3
  66.6 0.4 fusion.36
  67.3 1.5 fusion.63
  69.0 0.4 fusion.37
  69.4 0.9 subtract_bitcast_fusion.15
  70.5 0.8 add_dynamic-update-slice_fusion.22
  71.3 0.8 add_dynamic-update-slice_fusion.21
  72.1 0.8 add_dynamic-update-slice_fusion.20
  72.9 0.8 subtract_dynamic-update-slice_fusion.23
  73.8 0.8 subtract_dynamic-update-slice_fusion.22
  74.6 0.8 subtract_dynamic-update-slice_fusion.21
  75.3 0.8 subtract_dynamic-update-slice_fusion.20
  76.1 3.8 %all-to-all-start.2 = ((f32[8,2,128,256]{3,2,1,0:T(8,128)}), f32[8,2,128,256]{3,2,1,0:T(8,128)S(1)}, u32[]{:S(2)}, u32[]{:S(2)}) async-start(f32[8,2,128,256]{3,2,1,0:T(8,128)} %subtract_dynamic-update-slice_fusion.20), calls=%async_computation.2 | async-start | bytes 4194304 | tf_op jit(solution)/shard_map/all_to_all | solution.py:340
  80.0 0.3 fusion.221
  80.2 1.7 fusion.269
  82.2 0.7 fusion.91
  82.9 0.7 fusion.92
  83.6 0.7 fusion.93
  84.4 0.7 fusion.94
  85.1 0.7 fusion.95
  85.8 0.7 fusion.96
  86.5 0.7 fusion.97
  87.2 0.7 fusion.98
  88.0 18.4 %all-to-all-done.2 = f32[8,2,128,256]{3,2,1,0:T(8,128)S(1)} async-done(((f32[8,2,128,256]{3,2,1,0:T(8,128)}), f32[8,2,128,256]{3,2,1,0:T(8,128)S(1)}, u32[]{:S(2)}, u32[]{:S(2)}) %all-to-all-start.2) | async-done | bytes 2097184 | tf_op jit(solution)/shard_map/all_to_all | solution.py:340
  106.3 1.0 fusion.128
  107.6 0.3 fusion.38
  109.0 2.0 div.9
  112.4 2.4 fusion.40
  114.8 3.6 %all-to-all-start.3 = ((f32[8,2,128,256]{3,2,1,0:T(8,128)}), f32[8,2,128,256]{3,2,1,0:T(8,128)S(1)}, u32[]{:S(2)}, u32[]{:S(2)}) async-start(f32[8,2,128,256]{3,2,1,0:T(8,128)} %fusion.40), calls=%async_computation.3 | async-start | bytes 4194304 | tf_op jit(solution)/shard_map/all_to_all | solution.py:346
  118.4 0.3 all-reduce.5.cloned.1.call-start
  118.7 2.2 maximum_negate_fusion
  121.0 24.0 %all-to-all-done.3 = f32[8,2,128,256]{3,2,1,0:T(8,128)S(1)} async-done(((f32[8,2,128,256]{3,2,1,0:T(8,128)}), f32[8,2,128,256]{3,2,1,0:T(8,128)S(1)}, u32[]{:S(2)}, u32[]{:S(2)}) %all-to-all-start.3) | async-done | bytes 2097184 | tf_op jit(solution)/shard_map/all_to_all | solution.py:346
  146.3 0.4 fusion.44
  147.0 1.6 fusion.60
  148.8 1.0 copy-done.2
  149.8 0.4 fusion.45
  150.4 1.5 fusion.57
  152.2 0.4 fusion.46
  153.7 29.0 %all_to_all.25 = f32[8,2,128,256]{3,2,1,0:T(8,128)S(1)} all-to-all(f32[8,2,128,256]{3,2,1,0:T(8,128)S(1)} %subtract_dynamic-update-slice_fusion.4), channel_id=1, replica_groups=mesh['slab'=8,'view'=4] {'slab'}, dimensions={0} | all-to-all | bytes 4194304 | tf_op jit(solution)/shard_map/all_to_all | solution.py:340
  182.8 1.0 fusion.126
  184.0 0.3 fusion.47
  185.5 0.7 copy-done.5
  186.3 1.1 fusion.54
  187.9 1.5 copy.69
  189.3 86.0 %all-reduce.5.cloned.1.call-done = f32[4,128,1024]{2,1,0:T(8,128)} async-done(((f32[4,128,1024]{2,1,0:T(8,128)}), f32[4,128,1024]{2,1,0:T(8,128)}) %all-reduce.5.cloned.1.call-update) | async-done | bytes 2097168 | tf_op jit(solution)/shard_map/psum | solution.py:352
  275.4 3.3 %exponential_multiply_fusion = f32[4,128,1024]{2,1,0:T(8,128)} fusion(f32[4,128,1024]{2,1,0:T(8,128)S(1)} %copy-done.1, f32[4,128,1024]{2,1,0:T(8,128)} %all-reduce.5.cloned.1.call-done), kind=kLoop, calls=%fused_computation.69 | loop fusion | flops 1048576 | bytes 6291456 | tf_op jit(solution)/shard_map/mul | solution.py:353
  (213 shorter events, 14.9 us)
Async XLA Ops:
  9.5 7.0 %copy-start = (f32[4,128,1024]{2,1,0:T(8,128)S(1)}, f32[4,128,1024]{2,1,0:T(8,128)}, u32[]{:S(2)}) copy-start(f32[4,128,1024]{2,1,0:T(8,128)} %param.6) | copy-start | bytes 6291460
  11.1 20.6 %all-to-all-start.1 = ((f32[8,1,128,256]{3,2,1,0:T(8,128)}), f32[8,1,128,256]{3,2,1,0:T(8,128)S(1)}, u32[]{:S(2)}, u32[]{:S(2)}) async-start(f32[8,1,128,256]{3,2,1,0:T(8,128)} %convolution_bitcast_fusion), calls=%async_computation.1 | async-start | bytes 2097152 | tf_op jit(solution)/shard_map/all_to_all | solution.py:328
  16.5 0.7 copy-start.8
  16.6 0.7 copy-start.6
  17.3 0.7 copy-start.7
  18.8 1.1 copy-start.4
  31.7 30.2 %all-to-all-start = ((f32[8,2,128,256]{3,2,1,0:T(8,128)}), f32[8,2,128,256]{3,2,1,0:T(8,128)S(1)}, u32[]{:S(2)}, u32[]{:S(2)}) async-start(f32[8,2,128,256]{3,2,1,0:T(8,128)} %fusion.26), calls=%async_computation | async-start | bytes 4194304 | tf_op jit(solution)/shard_map/all_to_all | solution.py:328
  65.4 1.2 copy-start.3
  76.1 30.2 %all-to-all-start.2 = ((f32[8,2,128,256]{3,2,1,0:T(8,128)}), f32[8,2,128,256]{3,2,1,0:T(8,128)S(1)}, u32[]{:S(2)}, u32[]{:S(2)}) async-start(f32[8,2,128,256]{3,2,1,0:T(8,128)} %subtract_dynamic-update-slice_fusion.20), calls=%async_computation.2 | async-start | bytes 4194304 | tf_op jit(solution)/shard_map/all_to_all | solution.py:340
  114.8 30.2 %all-to-all-start.3 = ((f32[8,2,128,256]{3,2,1,0:T(8,128)}), f32[8,2,128,256]{3,2,1,0:T(8,128)S(1)}, u32[]{:S(2)}, u32[]{:S(2)}) async-start(f32[8,2,128,256]{3,2,1,0:T(8,128)} %fusion.40), calls=%async_computation.3 | async-start | bytes 4194304 | tf_op jit(solution)/shard_map/all_to_all | solution.py:346
  118.4 156.9 %all-reduce.5.cloned.1.call-start = ((), (), s32[]{:S(2)}) async-start(), calls=%async_computation.5 | async-start | bytes 4194304 | tf_op jit(solution)/shard_map/psum | solution.py:352
  148.5 1.2 copy-start.2
  185.2 1.0 copy-start.5
  189.3 86.0 %copy-start.1 = (f32[4,128,1024]{2,1,0:T(8,128)S(1)}, f32[4,128,1024]{2,1,0:T(8,128)}, u32[]{:S(2)}) copy-start(f32[4,128,1024]{2,1,0:T(8,128)} %param.6) | copy-start | bytes 6291460
Sparse Core Ops, SparseCore 0:
  189.5 85.8 all-reduce.4
where the time goes:
time: 286 us
  waiting for transfers between devices  158 us (55%)
  other arithmetic  38.9 us (14%)
  blocking collectives  29 us (10%)
  matrix products  17.6 us (6%)
  starting transfers between devices  16.7 us (6%)
  between operations  14.8 us (5%)
  local copies, waits for them, and re-layouts  9.96 us (3%)
    psum x1, waiting for transfers between devices, shards(): summed = lax.psum(log_terms, 'view')  86 us
    all_to_all x2, waiting for transfers between devices, to_columns_blocked(): lax.all_to_all(spectra, 'slab', split_axis=0, concat_axis=0, tiled=True)  30.1 us
    all_to_all x1, blocking collectives, convolve(): lax.all_to_all(planes, 'slab', split_axis=0, concat_axis=0, tiled=True)  29 us
    all_to_all x1, waiting for transfers between devices, shards(): lax.all_to_all(spectra, 'slab', split_axis=0, concat_axis=0, tiled=True)  24 us
    all_to_all x1, waiting for transfers between devices, convolve(): lax.all_to_all(planes, 'slab', split_axis=0, concat_axis=0, tiled=True)  18.4 us
    unnamed x82, other arithmetic  14.6 us
    all_to_all x2, starting transfers between devices, to_columns_blocked(): lax.all_to_all(spectra, 'slab', split_axis=0, concat_axis=0, tiled=True)  8.95 us
    dot_general x5, matrix products, lane_stage(): jnp.einsum('...j,jn->...n', joined, matrix, precision=lax.Precision.HIGH)  8.46 us
  transfers between devices with their start and end apart: 5, of which 5 were waited for; matrix products, arithmetic and copies ran while one was open for 7% of the time, Pallas kernels for 0%

commit v1 on v0

--- a/solution.py
+++ b/solution.py
@@ -5,6 +5,18 @@
 from jax.sharding import PartitionSpec as P
 
 highest = lax.Precision.HIGHEST
+
+
+def circles_remake(page, dim_no, s0):
+    v_next = page.shape
+    left_arr = page.reshape(*v_next[:dim_no], s0, v_next[dim_no] // s0, *v_next[dim_no + 1 :])
+    return jnp.moveaxis(left_arr, dim_no, 0)
+
+
+def fix_the_indices(my_data, ndim_at):
+    r_now = list(my_data.shape[1:])
+    r_now[ndim_at] *= my_data.shape[0]
+    return jnp.moveaxis(my_data, 0, ndim_at).reshape(r_now)
 
 
 def block_matrix(multiplier, shifting, weights):
@@ -343,7 +355,22 @@
     blurred = convolve(spectra, transfer_imag)
     quotient = to_blocks(views[0], block_count) / blurred
     spectra = depth_forward(quotient, depth)
-    spectra = lax.all_to_all(spectra, "slab", split_axis=0, concat_axis=0, tiled=True)
+
+    def pack_spots_all(a0, mesh_dim, piece_in, array_here):
+        w1 = lax.axis_size(mesh_dim)
+        z_new = lax.axis_index(mesh_dim)
+        vec_out, val = (w1, z_new)
+        t1 = circles_remake(a0, piece_in, vec_out)
+        buffers = [t1[val]]
+        for nth in range(1, vec_out):
+            latest = t1[val ^ nth]
+            o_now = lax.ppermute(latest, mesh_dim, [(m, m ^ nth) for m in range(vec_out)])
+            buffers.append(o_now)
+        z1 = jnp.stack(buffers)
+        t1 = z1[val ^ jnp.arange(vec_out)]
+        return fix_the_indices(t1, array_here)
+
+    spectra = pack_spots_all(spectra, "slab", 0, array_here=0)
     spectra = width_forward(spectra, width)
     smeared = convolve(spectra, -transfer_imag)
     correction = jnp.einsum("apxm,aml->apxl", smeared, doubled, precision=lax.Precision.HIGH)

time: 286 us -> 296 us (1.035)
  waiting for transfers between devices: 158 us -> 147 us
  other arithmetic: 38.9 us -> 49.8 us
  local copies, waits for them, and re-layouts: 9.96 us -> 18.6 us
    all_to_all x1 -> x0, waiting for transfers between devices: 24 us -> none  [shards(): lax.all_to_all(spectra, 'slab', split_axis=0, concat_axis=0, tiled=True)]
    ppermute x0 -> x7, waiting for transfers between devices: none -> 21.4 us  [pack_spots_all(): lax.ppermute(latest, mesh_dim, [(m, m ^ nth) for m in range(vec_out)])]
    all_to_all x2, waiting for transfers between devices: 30.1 us -> 22.4 us  [to_columns_blocked(): lax.all_to_all(spectra, 'slab', split_axis=0, concat_axis=0, tiled=True)]
    unnamed x26 -> x81, local copies, waits for them, and re-layouts: 4.88 us -> 9.97 us
    unnamed x82 -> x83, other arithmetic: 14.6 us -> 18.9 us
    ppermute x0 -> x7, starting transfers between devices: none -> 4.15 us  [pack_spots_all(): lax.ppermute(latest, mesh_dim, [(m, m ^ nth) for m in range(vec_out)])]
    all_to_all x1 -> x0, starting transfers between devices: 3.6 us -> none  [shards(): lax.all_to_all(spectra, 'slab', split_axis=0, concat_axis=0, tiled=True)]
  transfers between devices with their start and end apart: 5 -> 11, of which waited for: 5 -> 6; matrix products, arithmetic and copies ran while one was open for 7% -> 12% of each run, Pallas kernels for 0% -> 0%
where the time goes in v1:
time: 296 us; the launch traced here: 295 us
  waiting for transfers between devices  147 us (50%)
  other arithmetic  49.8 us (17%)
  blocking collectives  29 us (10%)
  local copies, waits for them, and re-layouts  18.6 us (6%)
  matrix products  17.9 us (6%)
  starting transfers between devices  17.4 us (6%)
  between operations  15.1 us (5%)
    psum x1, waiting for transfers between devices, shards(): summed = lax.psum(log_terms, 'view')  86 us
    all_to_all x1, blocking collectives, convolve(): lax.all_to_all(planes, 'slab', split_axis=0, concat_axis=0, tiled=True)  29 us
    all_to_all x2, waiting for transfers between devices, to_columns_blocked(): lax.all_to_all(spectra, 'slab', split_axis=0, concat_axis=0, tiled=True)  22.4 us
    ppermute x7, waiting for transfers between devices, pack_spots_all(): lax.ppermute(latest, mesh_dim, [(m, m ^ nth) for m in range(vec_out)])  21.4 us
    unnamed x83, other arithmetic  18.9 us
    all_to_all x1, waiting for transfers between devices, convolve(): lax.all_to_all(planes, 'slab', split_axis=0, concat_axis=0, tiled=True)  17.2 us
    unnamed x81, local copies, waits for them, and re-layouts  9.97 us
    all_to_all x2, starting transfers between devices, to_columns_blocked(): lax.all_to_all(spectra, 'slab', split_axis=0, concat_axis=0, tiled=True)  9.36 us
  transfers between devices with their start and end apart: 11, of which 6 were waited for; matrix products, arithmetic and copies ran while one was open for 12% of the time, Pallas kernels for 0%

profile of v1, /device:TPU:0, one launch (start us, length us, event | category | flops | bytes accessed | tf_op | source)
XLA Modules:
  0.0 294.8 jit_solution(15101042439127880588)
XLA Ops:
  7.2 1.3 copy.41
  9.6 1.6 convolution_bitcast_fusion
  11.2 5.2 %all-to-all-start.1 = ((f32[8,1,128,256]{3,2,1,0:T(8,128)}), f32[8,1,128,256]{3,2,1,0:T(8,128)S(1)}, u32[]{:S(2)}, u32[]{:S(2)}) async-start(f32[8,1,128,256]{3,2,1,0:T(8,128)} %convolution_bitcast_fusion), calls=%async_computation.1 | async-start | bytes 2097152 | tf_op jit(solution)/shard_map/all_to_all | solution.py:340
  16.4 0.9 fusion.219
  19.5 1.0 fusion.52
  20.6 0.8 subtract_bitcast_fusion.21
  21.8 0.8 constant_dynamic-update-slice_fusion.6
  22.6 0.8 constant_dynamic-update-slice_fusion.5
  23.3 0.8 constant_dynamic-update-slice_fusion.4
  24.1 0.8 constant_dynamic-update-slice_fusion.3
  24.9 0.8 constant_dynamic-update-slice_fusion.2
  25.8 0.8 constant_dynamic-update-slice_fusion.1
  27.1 2.0 constant_dynamic-update-slice_fusion
  29.1 1.7 slice_negate_fusion.13
  30.9 4.0 %fusion.26 = f32[8,2,128,256]{3,2,1,0:T(8,128)} fusion(f32[8,2,128,128]{3,2,1,0:T(8,128)S(1)} %get-tuple-element.152, f32[8,2,128,128]{3,2,1,0:T(8,128)S(1)} %get-tuple-element.151, f32[8,2,128,256]{3,2,1,0:T(8,128)} %constant_dynamic-update-slice_fusion, f32[8,256]{1,0:T(8,128)S(1)} %copy-done.23, f32[8,256]{1,0:T(8,128)S(1)} %get-tuple-element.355, ...), kind=kOutput, calls=%fused_computation.39 | convolution fusion | flops 807600128 | bytes 6504448 | tf_op jit(solution)/shard_map/...j,jn->...n/dot_general | solution.py:247
  34.9 4.2 %all-to-all-start = ((f32[8,2,128,256]{3,2,1,0:T(8,128)}), f32[8,2,128,256]{3,2,1,0:T(8,128)S(1)}, u32[]{:S(2)}, u32[]{:S(2)}) async-start(f32[8,2,128,256]{3,2,1,0:T(8,128)} %fusion.26), calls=%async_computation | async-start | bytes 4194304 | tf_op jit(solution)/shard_map/all_to_all | solution.py:340
  40.4 0.9 fusion.70
  41.2 1.0 slice_bitcast_fusion.67
  42.3 1.0 maximum_bitcast_fusion.7
  43.3 22.4 %all-to-all-done = f32[8,2,128,256]{3,2,1,0:T(8,128)S(1)} async-done(((f32[8,2,128,256]{3,2,1,0:T(8,128)}), f32[8,2,128,256]{3,2,1,0:T(8,128)S(1)}, u32[]{:S(2)}, u32[]{:S(2)}) %all-to-all-start) | async-done | bytes 2097184 | tf_op jit(solution)/shard_map/all_to_all | solution.py:340
  67.7 1.6 fusion.66
  69.5 1.0 copy-done.3
  71.7 1.5 fusion.63
  74.3 0.8 subtract_bitcast_fusion.15
  75.4 0.8 constant_dynamic-update-slice_fusion.46
  76.2 0.8 constant_dynamic-update-slice_fusion.45
  77.0 0.8 constant_dynamic-update-slice_fusion.44
  77.8 0.8 constant_dynamic-update-slice_fusion.43
  78.6 0.8 constant_dynamic-update-slice_fusion.42
  79.4 0.8 constant_dynamic-update-slice_fusion.41
  80.2 0.8 constant_dynamic-update-slice_fusion.40
  81.0 3.6 %all-to-all-start.2 = ((f32[8,2,128,256]{3,2,1,0:T(8,128)}), f32[8,2,128,256]{3,2,1,0:T(8,128)S(1)}, u32[]{:S(2)}, u32[]{:S(2)}) async-start(f32[8,2,128,256]{3,2,1,0:T(8,128)} %constant_dynamic-update-slice_fusion.40), calls=%async_computation.2 | async-start | bytes 4194304 | tf_op jit(solution)/shard_map/all_to_all | solution.py:352
  86.2 1.7 fusion.270
  88.2 0.7 fusion.91
  88.9 0.7 fusion.92
  89.6 0.7 fusion.93
  90.3 0.7 fusion.94
  91.1 0.7 fusion.95
  91.8 0.7 fusion.96
  93.2 0.7 fusion.98
  93.9 17.2 %all-to-all-done.2 = f32[8,2,128,256]{3,2,1,0:T(8,128)S(1)} async-done(((f32[8,2,128,256]{3,2,1,0:T(8,128)}), f32[8,2,128,256]{3,2,1,0:T(8,128)S(1)}, u32[]{:S(2)}, u32[]{:S(2)}) %all-to-all-start.2) | async-done | bytes 2097184 | tf_op jit(solution)/shard_map/all_to_all | solution.py:352
  111.2 1.0 fusion.128
  114.3 2.0 div.9
  118.3 1.1 fusion.40
  119.4 1.3 constant_dynamic-slice_fusion
  120.7 2.4 maximum_negate_fusion
  123.7 1.4 collective-permute-start.2
  125.6 1.1 collective-permute-start.4
  127.3 1.0 constant_dynamic-update-slice_fusion.70
  128.2 4.1 %collective-permute-done.1 = f32[1,2,128,256]{3,2,1,0:T(8,128)S(1)} collective-permute-done((f32[1,2,128,256]{3,2,1,0:T(8,128)}, f32[1,2,128,256]{3,2,1,0:T(8,128)S(1)}, u32[]{:S(2)}, u32[]{:S(2)}) %collective-permute-start.1) | collective-permute-done | bytes 262176 | tf_op jit(solution)/shard_map/ppermute | solution.py:367
  132.4 4.8 %collective-permute-done.2 = f32[1,2,128,256]{3,2,1,0:T(8,128)S(1)} collective-permute-done((f32[1,2,128,256]{3,2,1,0:T(8,128)S(1)}, f32[1,2,128,256]{3,2,1,0:T(8,128)S(1)}, u32[]{:S(2)}, u32[]{:S(2)}) %collective-permute-start.2) | collective-permute-done | bytes 262176 | tf_op jit(solution)/shard_map/ppermute | solution.py:367
  137.3 12.4 %collective-permute-done.4 = f32[1,2,128,256]{3,2,1,0:T(8,128)S(1)} collective-permute-done((f32[1,2,128,256]{3,2,1,0:T(8,128)S(1)}, f32[1,2,128,256]{3,2,1,0:T(8,128)S(1)}, u32[]{:S(2)}, u32[]{:S(2)}) %collective-permute-start.4) | collective-permute-done | bytes 262176 | tf_op jit(solution)/shard_map/ppermute | solution.py:367
  149.9 1.3 copy-done.8
  151.2 2.3 gather_fusion
  155.4 1.6 fusion.60
  157.2 1.0 copy-done.2
  158.8 1.5 fusion.57
  162.6 29.0 %all_to_all.20 = f32[8,2,128,256]{3,2,1,0:T(8,128)S(1)} all-to-all(f32[8,2,128,256]{3,2,1,0:T(8,128)S(1)} %constant_dynamic-update-slice_fusion.80), channel_id=1, replica_groups=mesh['slab'=8,'view'=4] {'slab'}, dimensions={0} | all-to-all | bytes 4194304 | tf_op jit(solution)/shard_map/all_to_all | solution.py:352
  191.6 1.0 fusion.126
  194.8 0.7 copy-done.16
  195.5 1.1 fusion.54
  197.1 1.5 copy.69
  198.6 86.0 %all-reduce.5.cloned.1.call-done = f32[4,128,1024]{2,1,0:T(8,128)} async-done(((f32[4,128,1024]{2,1,0:T(8,128)}), f32[4,128,1024]{2,1,0:T(8,128)}) %all-reduce.5.cloned.1.call-update) | async-done | bytes 2097168 | tf_op jit(solution)/shard_map/psum | solution.py:379
  284.7 3.3 %exponential_multiply_fusion = f32[4,128,1024]{2,1,0:T(8,128)} fusion(f32[4,128,1024]{2,1,0:T(8,128)S(1)} %copy-done.1, f32[4,128,1024]{2,1,0:T(8,128)} %all-reduce.5.cloned.1.call-done), kind=kLoop, calls=%fused_computation.70 | loop fusion | flops 1048576 | bytes 6291456 | tf_op jit(solution)/shard_map/mul | solution.py:380
  (285 shorter events, 26.1 us)
Async XLA Ops:
  7.2 2.4 copy-start.12
  9.5 1.7 copy-start.22
  9.5 7.7 %copy-start = (f32[4,128,1024]{2,1,0:T(8,128)S(1)}, f32[4,128,1024]{2,1,0:T(8,128)}, u32[]{:S(2)}) copy-start(f32[4,128,1024]{2,1,0:T(8,128)} %param.6) | copy-start | bytes 6291460
  11.2 23.7 %all-to-all-start.1 = ((f32[8,1,128,256]{3,2,1,0:T(8,128)}), f32[8,1,128,256]{3,2,1,0:T(8,128)S(1)}, u32[]{:S(2)}, u32[]{:S(2)}) async-start(f32[8,1,128,256]{3,2,1,0:T(8,128)} %convolution_bitcast_fusion), calls=%async_computation.1 | async-start | bytes 2097152 | tf_op jit(solution)/shard_map/all_to_all | solution.py:340
  17.3 0.7 copy-start.32
  17.3 0.7 copy-start.29
  18.0 0.7 copy-start.30
  19.5 1.1 copy-start.15
  21.5 3.5 %copy-start.4 = (f32[1,2,128,128]{3,2,1,0:T(8,128)}, f32[1,2,128,128]{3,2,1,0:T(8,128)S(1)}, u32[]{:S(2)}) copy-start(f32[1,2,128,128]{3,2,1,0:T(8,128)S(1)} %get-tuple-element.303) | copy-start | bytes 393220
  21.5 3.4 %copy-start.5 = (f32[1,2,128,128]{3,2,1,0:T(8,128)}, f32[1,2,128,128]{3,2,1,0:T(8,128)S(1)}, u32[]{:S(2)}) copy-start(f32[1,2,128,128]{3,2,1,0:T(8,128)S(1)} %get-tuple-element.304) | copy-start | bytes 393220
  21.7 3.3 %copy-start.6 = (f32[1,2,128,128]{3,2,1,0:T(8,128)}, f32[1,2,128,128]{3,2,1,0:T(8,128)S(1)}, u32[]{:S(2)}) copy-start(f32[1,2,128,128]{3,2,1,0:T(8,128)S(1)} %get-tuple-element.309) | copy-start | bytes 393220
  21.7 3.3 %copy-start.7 = (f32[1,2,128,128]{3,2,1,0:T(8,128)}, f32[1,2,128,128]{3,2,1,0:T(8,128)S(1)}, u32[]{:S(2)}) copy-start(f32[1,2,128,128]{3,2,1,0:T(8,128)S(1)} %get-tuple-element.310) | copy-start | bytes 393220
  21.7 2.4 copy-start.10
  21.8 2.4 copy-start.11
  29.1 1.7 copy-start.13
  29.1 1.7 copy-start.23
  34.9 30.8 %all-to-all-start = ((f32[8,2,128,256]{3,2,1,0:T(8,128)}), f32[8,2,128,256]{3,2,1,0:T(8,128)S(1)}, u32[]{:S(2)}, u32[]{:S(2)}) async-start(f32[8,2,128,256]{3,2,1,0:T(8,128)} %fusion.26), calls=%async_computation | async-start | bytes 4194304 | tf_op jit(solution)/shard_map/all_to_all | solution.py:340
  69.3 1.2 copy-start.3
  70.9 0.8 copy-start.9
  73.2 0.7 copy-start.27
  81.0 30.2 %all-to-all-start.2 = ((f32[8,2,128,256]{3,2,1,0:T(8,128)}), f32[8,2,128,256]{3,2,1,0:T(8,128)S(1)}, u32[]{:S(2)}, u32[]{:S(2)}) async-start(f32[8,2,128,256]{3,2,1,0:T(8,128)} %constant_dynamic-update-slice_fusion.40), calls=%async_computation.2 | async-start | bytes 4194304 | tf_op jit(solution)/shard_map/all_to_all | solution.py:352
  84.6 200.1 %all-reduce.5.cloned.1.call-start = ((), (), s32[]{:S(2)}) async-start(), calls=%async_computation.4 | async-start | bytes 4194304 | tf_op jit(solution)/shard_map/psum | solution.py:379
  112.2 0.7 copy-start.25
  117.5 0.8 copy-start.14
  117.5 0.8 copy-start.24
  119.4 1.3 copy-start.31
  120.7 6.0 %collective-permute-start = (f32[1,2,128,256]{3,2,1,0:T(8,128)}, f32[1,2,128,256]{3,2,1,0:T(8,128)}, u32[]{:S(2)}, u32[]{:S(2)}) collective-permute-start(f32[1,2,128,256]{3,2,1,0:T(8,128)} %get-tuple-element.112), channel_id=1, source_target_pairs={{0,4},{4,0},{8,12},{12,8},{16,20},{20,16},{24,28},{28,24},{1,5},{5... | collective-permute-start | bytes 786440 | tf_op jit(solution)/shard_map/ppermute | solution.py:367
  120.7 3.0 %copy-start.21 = (f32[1,2,128,256]{3,2,1,0:T(8,128)S(1)}, f32[1,2,128,256]{3,2,1,0:T(8,128)}, u32[]{:S(2)}) copy-start(f32[1,2,128,256]{3,2,1,0:T(8,128)} %get-tuple-element.110) | copy-start | bytes 786436
  120.7 4.4 %copy-start.20 = (f32[1,2,128,256]{3,2,1,0:T(8,128)S(1)}, f32[1,2,128,256]{3,2,1,0:T(8,128)}, u32[]{:S(2)}) copy-start(f32[1,2,128,256]{3,2,1,0:T(8,128)} %get-tuple-element.109) | copy-start | bytes 786436
  120.7 4.9 %copy-start.19 = (f32[1,2,128,256]{3,2,1,0:T(8,128)S(1)}, f32[1,2,128,256]{3,2,1,0:T(8,128)}, u32[]{:S(2)}) copy-start(f32[1,2,128,256]{3,2,1,0:T(8,128)} %get-tuple-element.108) | copy-start | bytes 786436
  120.7 6.0 %copy-start.18 = (f32[1,2,128,256]{3,2,1,0:T(8,128)S(1)}, f32[1,2,128,256]{3,2,1,0:T(8,128)}, u32[]{:S(2)}) copy-start(f32[1,2,128,256]{3,2,1,0:T(8,128)} %get-tuple-element.107) | copy-start | bytes 786436
  120.7 11.7 %copy-start.17 = (f32[1,2,128,256]{3,2,1,0:T(8,128)S(1)}, f32[1,2,128,256]{3,2,1,0:T(8,128)}, u32[]{:S(2)}) copy-start(f32[1,2,128,256]{3,2,1,0:T(8,128)} %get-tuple-element.106) | copy-start | bytes 786436
  123.1 9.3 %collective-permute-start.1 = (f32[1,2,128,256]{3,2,1,0:T(8,128)}, f32[1,2,128,256]{3,2,1,0:T(8,128)S(1)}, u32[]{:S(2)}, u32[]{:S(2)}) collective-permute-start(f32[1,2,128,256]{3,2,1,0:T(8,128)} %get-tuple-element.111), channel_id=1, source_target_pairs={{0,8},{4,12},{8,0},{12,4},{16,24},{20,28},{24,16},{28,20},{1,9},{5... | collective-permute-start | bytes 786440 | tf_op jit(solution)/shard_map/ppermute | solution.py:367
  123.7 13.6 %collective-permute-start.2 = (f32[1,2,128,256]{3,2,1,0:T(8,128)S(1)}, f32[1,2,128,256]{3,2,1,0:T(8,128)S(1)}, u32[]{:S(2)}, u32[]{:S(2)}) collective-permute-start(f32[1,2,128,256]{3,2,1,0:T(8,128)S(1)} %copy-done.21), channel_id=1, source_target_pairs={{0,12},{4,8},{8,4},{12,0},{16,28},{20,24},{24,20},{28,16},{1,13},{... | collective-permute-start | bytes 786440 | tf_op jit(solution)/shard_map/ppermute | solution.py:367
  125.0 12.2 %collective-permute-start.3 = (f32[1,2,128,256]{3,2,1,0:T(8,128)S(1)}, f32[1,2,128,256]{3,2,1,0:T(8,128)S(1)}, u32[]{:S(2)}, u32[]{:S(2)}) collective-permute-start(f32[1,2,128,256]{3,2,1,0:T(8,128)S(1)} %copy-done.20), channel_id=1, source_target_pairs={{0,16},{4,20},{8,24},{12,28},{16,0},{20,4},{24,8},{28,12},{1,17},{... | collective-permute-start | bytes 786440 | tf_op jit(solution)/shard_map/ppermute | solution.py:367
  125.6 24.2 %collective-permute-start.4 = (f32[1,2,128,256]{3,2,1,0:T(8,128)S(1)}, f32[1,2,128,256]{3,2,1,0:T(8,128)S(1)}, u32[]{:S(2)}, u32[]{:S(2)}) collective-permute-start(f32[1,2,128,256]{3,2,1,0:T(8,128)S(1)} %copy-done.19), channel_id=1, source_target_pairs={{0,20},{4,16},{8,28},{12,24},{16,4},{20,0},{24,12},{28,8},{1,21},{... | collective-permute-start | bytes 786440 | tf_op jit(solution)/shard_map/ppermute | solution.py:367
  126.7 23.1 %collective-permute-start.5 = (f32[1,2,128,256]{3,2,1,0:T(8,128)S(1)}, f32[1,2,128,256]{3,2,1,0:T(8,128)S(1)}, u32[]{:S(2)}, u32[]{:S(2)}) collective-permute-start(f32[1,2,128,256]{3,2,1,0:T(8,128)S(1)} %copy-done.18), channel_id=1, source_target_pairs={{0,24},{4,28},{8,16},{12,20},{16,8},{20,12},{24,0},{28,4},{1,25},{... | collective-permute-start | bytes 786440 | tf_op jit(solution)/shard_map/ppermute | solution.py:367
  132.4 17.4 %collective-permute-start.6 = (f32[1,2,128,256]{3,2,1,0:T(8,128)S(1)}, f32[1,2,128,256]{3,2,1,0:T(8,128)S(1)}, u32[]{:S(2)}, u32[]{:S(2)}) collective-permute-start(f32[1,2,128,256]{3,2,1,0:T(8,128)S(1)} %copy-done.17), channel_id=1, source_target_pairs={{0,28},{4,24},{8,20},{12,16},{16,12},{20,8},{24,4},{28,0},{1,29},{... | collective-permute-start | bytes 786440 | tf_op jit(solution)/shard_map/ppermute | solution.py:367
  149.8 1.3 copy-start.8
  156.9 1.2 copy-start.2
  160.3 0.7 copy-start.28
  192.6 0.7 copy-start.26
  194.5 1.0 copy-start.16
  198.6 86.1 %copy-start.1 = (f32[4,128,1024]{2,1,0:T(8,128)S(1)}, f32[4,128,1024]{2,1,0:T(8,128)}, u32[]{:S(2)}) copy-start(f32[4,128,1024]{2,1,0:T(8,128)} %param.6) | copy-start | bytes 6291460
Sparse Core Ops, SparseCore 0:
  198.7 85.8 all-reduce.4
